TPU v7x, 512 devices: a whole 4x8x8 slice. The times are simulated.
512 devices in a mesh: dp: 64 (over z, x, core), mp: 8 (over y).
Axes of the slice: x: 4, y: 8, z: 8, core: 2. Of those that a mesh axis runs over, the one named last changes fastest.
Arguments:
- micro_grads: bfloat16 [64, 2, 768, 768], P('dp', None, None, 'mp'), may hold values from -16 to 16
- master: float32 [768, 768], P('dp', 'mp'), may hold values from -0.21875 to 0.21875
- moment: float32 [768, 768], P('dp', 'mp'), may hold values from -1.5 to 1.5
- second: float32 [768, 768], P('dp', 'mp'), may hold values from 0.001 to 0.1
- left_basis: float32 [768, 768], P(None, 'dp'), may hold values from -0.21875 to 0.21875
- right_basis: float32 [768, 768], P(None, 'mp'), may hold values from -0.21875 to 0.21875
- left_stat: float32 [768, 768], P('mp'), may hold values from -2 to 5, as said below
- right_stat: float32 [768, 768], P('mp'), may hold values from -2 to 5, as said below
Outputs:
- weights_block: bfloat16 [768, 768], P(None, 'mp')
- new_master: float32 [768, 768], P('dp', 'mp')
- new_moment: float32 [768, 768], P('dp', 'mp')
- new_second: float32 [768, 768], P('dp', 'mp')
- new_left_stat: float32 [768, 768], P('mp')
- new_right_stat: float32 [768, 768], P('mp')
- new_left_basis: float32 [768, 768], P('mp')
- new_right_basis: float32 [768, 768], P('mp')
Inputs may be any that keep to these rules, and one draw needn't show every extreme that they name: `left_stat`: symmetric. `right_stat`: symmetric.
All inputs are finite; a program needn't handle non-finite values.
Results may differ from a plain program's by a relative error of at most 0.004.
The roundings to bfloat16 on the way count: a program that leaves them out, or rounds other values in their place, can miss the bound.
Values may be sent and summed in bfloat16 or wider, within the bound.
No kernel may reach another device: no remote copies, remote signals or barrier semaphores. Data moves between devices by JAX's collectives and lax.ppermute only.
A program may use at most 64 MiB of HBM per device.

v0:
```python
import jax
import jax.numpy as jnp
from jax import lax
from jax.sharding import PartitionSpec as P

beta_one = 0.9
beta_two = 0.95
beta_stat = 0.95
learn_rate = 0.02
adam_eps = 1e-08
norm_eps = 1e-06
quint_a = 1.875
quint_b = -1.25
quint_c = 0.375
highest = lax.Precision.HIGHEST


def for_sending(x):

    def short(part):
        return part.astype(jnp.bfloat16) if part.dtype == jnp.float32 else part

    return jax.tree.map(short, x)


def all_rows(pair):
    return jax.tree.map(
        lambda part, own: part.astype(own.dtype),
        lax.all_gather(for_sending(pair), "mp", axis=0, tiled=True),
        pair,
    )


def row_gram(row_part, whole_part):
    return lax.dot_general(
        row_part, whole_part, (((1,), (1,)), ((), ())), preferred_element_type=jnp.float32
    )


def scatter_sum(x, axis):
    count = lax.axis_size(axis)
    chunks = x.reshape((count, x.shape[0] // count) + x.shape[1:])
    return jnp.sum(lax.all_to_all(chunks, axis, 0, 0, tiled=False), axis=0)


def gather_rows(x, axis):
    count = lax.axis_size(axis)
    return lax.all_to_all(jnp.broadcast_to(x[None], (count,) + x.shape), axis, 0, 0, tiled=False)


def per_device(micro_grads, master, moment, second, left_basis, right_basis, left_stat, right_stat):
    dp_count = lax.axis_size("dp")
    micro_count = micro_grads.shape[1]
    local_sum = jnp.sum(micro_grads[0], axis=0, dtype=jnp.float32)
    grad_piece = scatter_sum(local_sum, "dp") / (micro_count * dp_count)
    new_moment = beta_one * moment + (1.0 - beta_one) * grad_piece
    pieces = gather_rows(jnp.stack([grad_piece, new_moment]), "dp")
    pieces = jnp.swapaxes(pieces, 0, 1).reshape(2, -1, pieces.shape[-1])
    left_full = lax.all_gather(left_basis, "dp", axis=1, tiled=True)
    both_full = lax.all_gather(pieces, "mp", axis=2, tiled=True)
    right_full = lax.all_gather(right_basis, "mp", axis=1, tiled=True)
    grad_full = both_full[0]
    moment_full = both_full[1]

    def rotate(matrix):
        left_part = lax.dot_general(left_basis, matrix, (((0,), (0,)), ((), ())), precision=highest)
        return jnp.dot(left_part, right_basis, precision=highest)

    rot_grad = rotate(grad_full)
    rot_moment = rotate(moment_full)
    new_second = beta_two * second + (1.0 - beta_two) * rot_grad * rot_grad
    rot_step = rot_moment / (jnp.sqrt(new_second) + adam_eps)
    back_half = scatter_sum(
        lax.dot_general(right_basis, rot_step, (((1,), (1,)), ((), ())), precision=highest), "mp"
    )
    step_piece = scatter_sum(
        lax.dot_general(left_basis, back_half, (((1,), (1,)), ((), ())), precision=highest), "dp"
    )
    new_master = master - learn_rate * step_piece
    weights_block = gather_rows(new_master.astype(jnp.bfloat16), "dp").reshape(
        -1, new_master.shape[1]
    )
    band_width = right_basis.shape[1]
    band_start = lax.axis_index("mp") * band_width
    grad_band = lax.dynamic_slice_in_dim(grad_full, band_start, band_width, 0)
    grad_strip = lax.dynamic_slice_in_dim(grad_full, band_start, band_width, 1)
    left_outer = lax.dot_general(grad_band, grad_full, (((1,), (1,)), ((), ())), precision=highest)
    right_outer = lax.dot_general(
        grad_strip, grad_full, (((0,), (0,)), ((), ())), precision=highest
    )
    new_left_stat = beta_stat * left_stat + (1.0 - beta_stat) * left_outer
    new_right_stat = beta_stat * right_stat + (1.0 - beta_stat) * right_outer
    order_count = left_stat.shape[1]
    power_left = jnp.dot(
        new_left_stat.astype(jnp.bfloat16),
        left_full.astype(jnp.bfloat16),
        preferred_element_type=jnp.float32,
    )
    power_right = jnp.dot(
        new_right_stat.astype(jnp.bfloat16),
        right_full.astype(jnp.bfloat16),
        preferred_element_type=jnp.float32,
    )
    total_left, total_right = lax.psum(
        (jnp.sum(power_left * power_left), jnp.sum(power_right * power_right)), "mp"
    )
    start_left = lax.optimization_barrier(
        (power_left * lax.rsqrt(total_left * (4.0 / order_count) + norm_eps)).astype(jnp.bfloat16)
    )
    start_right = lax.optimization_barrier(
        (power_right * lax.rsqrt(total_right * (4.0 / order_count) + norm_eps)).astype(jnp.bfloat16)
    )
    start_rows = (start_left, start_right)
    start_whole = all_rows(start_rows)
    gram_rows = tuple(
        (
            lax.optimization_barrier(row_gram(row_part, whole_part).astype(jnp.bfloat16))
            for row_part, whole_part in zip(start_rows, start_whole)
        )
    )
    gram_whole = all_rows(gram_rows)
    middle_rows = []
    for row_part, gram_part, gram_all, whole_part in zip(
        start_rows, gram_rows, gram_whole, start_whole
    ):
        square = jnp.dot(gram_part, gram_all, preferred_element_type=jnp.float32)
        poly_rows = (quint_b * gram_part.astype(jnp.float32) + quint_c * square).astype(
            jnp.bfloat16
        )
        middle = quint_a * row_part.astype(jnp.float32) + jnp.dot(
            poly_rows, whole_part, preferred_element_type=jnp.float32
        )
        middle_rows.append(lax.optimization_barrier(middle.astype(jnp.bfloat16)))
    middle_whole = all_rows(tuple(middle_rows))
    new_bases = []
    for row_part, whole_part in zip(middle_rows, middle_whole):
        gram_two = row_gram(row_part, whole_part).astype(jnp.bfloat16)
        new_bases.append(
            1.5 * row_part.astype(jnp.float32)
            - 0.5 * jnp.dot(gram_two, whole_part, preferred_element_type=jnp.float32)
        )
    return (
        weights_block,
        new_master,
        new_moment,
        new_second,
        new_left_stat,
        new_right_stat,
        new_bases[0],
        new_bases[1],
    )


def solution(mesh):
    in_specs = (
        P("dp", None, None, "mp"),
        P("dp", "mp"),
        P("dp", "mp"),
        P("dp", "mp"),
        P(None, "dp"),
        P(None, "mp"),
        P("mp", None),
        P("mp", None),
    )
    out_specs = (
        P(None, "mp"),
        P("dp", "mp"),
        P("dp", "mp"),
        P("dp", "mp"),
        P("mp", None),
        P("mp", None),
        P("mp", None),
        P("mp", None),
    )
    return jax.shard_map(
        per_device, mesh=mesh, in_specs=in_specs, out_specs=out_specs, check_vma=False
    )
```

profile of v0, /device:TPU:2, one launch (start us, length us, event | category | flops | bytes accessed | tf_op | source)
XLA Modules:
  0.0 490.6 jit_solution(16406727266121706216)
XLA Ops:
  7.2 0.0 all-gather.27.cloned.1.call-start
  7.2 1.4 bitcast_convert_fusion
  8.6 0.0 all-gather.11.cloned.1.call-start
  8.7 1.0 convert_reduce_fusion
  9.7 0.2 copy.20
  10.0 31.4 %all_to_all.25 = f32[64,12,96]{2,1,0:T(8,128)S(1)} all-to-all(f32[64,12,96]{2,1,0:T(8,128)S(1)} %reshape.45), channel_id=1, replica_groups=mesh['dp'=64,'mp'=8] {'dp'}, dimensions={0} | all-to-all | bytes 589824 | tf_op jit(solution)/shard_map/all_to_all | solution.py:43
  41.3 0.1 reduce_sum.55
  41.5 0.2 broadcast_in_dim.4
  41.7 28.9 %all_to_all.26 = f32[64,2,12,96]{3,1,2,0:T(2,128)S(1)} all-to-all(f32[64,2,12,96]{3,1,2,0:T(2,128)S(1)} %broadcast_in_dim.4), channel_id=1, replica_groups=mesh['dp'=64,'mp'=8] {'dp'}, dimensions={0} | all-to-all | bytes 1179648 | tf_op jit(solution)/shard_map/all_to_all | solution.py:48
  70.6 1.2 copy.22
  71.7 0.0 all-gather.19.cloned.1.call-start
  71.8 0.7 convert.1
  72.5 0.0 all-gather.19.cloned.1.call-update
  72.5 0.2 all-gather.21.cloned.1.call-start
  72.7 27.0 %all-gather.27.cloned.1.call-done = bf16[64,12,768]{2,1,0:T(8,128)(2,1)} async-done(((bf16[1,12,768]{2,1,0:T(8,128)(2,1)}), bf16[64,12,768]{2,1,0:T(8,128)(2,1)}) %all-gather.27.cloned.1.call-update) | async-done | bytes 1179664 | tf_op jit(solution)/shard_map/all_gather | solution.py:59
  99.7 3.1 reshape.52
  102.9 59.1 %all-gather.11.cloned.1.call-done = f32[2,768,768]{1,0,2:T(2,128)} async-done(((f32[2,768,96]{1,0,2:T(2,128)}), f32[2,768,768]{1,0,2:T(2,128)}) %all-gather.11.cloned.1.call-update) | async-done | bytes 4718608 | tf_op jit(solution)/shard_map/all_gather | solution.py:60
  162.0 9.3 %fusion.53 = (f32[1,768,768]{1,0,2:T(1,128)S(1)}, f32[1,768,768]{1,0,2:T(1,128)}) fusion(f32[2,768,768]{1,0,2:T(2,128)} %all-gather.11.cloned.1.call-done), kind=kLoop, calls=%fused_computation.70 | loop fusion | bytes 9437184 | tf_op jit(solution)/shard_map/slice | solution.py:62
  171.3 0.1 constant_dynamic-slice_fusion
  171.4 0.9 constant_dynamic-slice_fusion.1
  172.3 1.5 fusion.23
  173.8 1.8 multiply_reduce_fusion.1
  175.7 2.4 fusion.20
  178.1 27.0 %all-gather.19.cloned.1.call-done = bf16[768,768]{0,1:T(8,128)(2,1)} async-done(((bf16[768,96]{0,1:T(8,128)(2,1)}), bf16[768,768]{0,1:T(8,128)(2,1)}) %all-gather.19.cloned.1.call-update) | async-done | bytes 1179664 | tf_op jit(solution)/shard_map/all_gather | solution.py:61
  205.1 2.4 multiply_reduce_fusion
  207.5 16.5 %all-reduce = (f32[]{:T(128)}, f32[]{:T(128)}) all-reduce(f32[]{:T(128)} %get-tuple-element.32, f32[]{:T(128)} %get-tuple-element.34), channel_id=1, replica_groups=mesh['dp'=64,'mp'=8] {'mp'}, use_global_device_ids=true, to_apply=%region_5.0 | all-reduce | flops 2 | bytes 16 | tf_op jit(solution)/shard_map/psum | solution.py:104
  224.8 0.7 multiply_convert_fusion
  225.4 0.0 all-gather.21.cloned.1.call-update
  225.5 0.0 all-gather.13.cloned.1.call-start
  226.2 0.7 multiply_convert_fusion.1
  226.9 0.0 all-gather.13.cloned.1.call-update
  226.9 0.0 all-gather.23.cloned.1.call-start
  227.0 39.7 %all-gather.21.cloned.1.call-done = bf16[768,768]{1,0:T(8,128)(2,1)} async-done(((bf16[96,768]{1,0:T(8,128)(2,1)}), bf16[768,768]{1,0:T(8,128)(2,1)}) %all-gather.21.cloned.1.call-update) | async-done | bytes 1179664 | tf_op jit(solution)/shard_map/all_gather | solution.py:29
  266.7 2.5 convolution_convert_fusion.1
  269.3 0.0 all-gather.23.cloned.1.call-update
  269.3 0.0 all-gather.15.cloned.1.call-start
  269.3 40.1 %all-gather.13.cloned.1.call-done = bf16[768,768]{1,0:T(8,128)(2,1)} async-done(((bf16[96,768]{1,0:T(8,128)(2,1)}), bf16[768,768]{1,0:T(8,128)(2,1)}) %all-gather.13.cloned.1.call-update) | async-done | bytes 1179664 | tf_op jit(solution)/shard_map/all_gather | solution.py:29
  309.5 2.4 convolution_convert_fusion.3
  312.0 0.0 all-gather.25.cloned.1.call-start
  312.0 40.2 %all-gather.23.cloned.1.call-done = bf16[768,768]{1,0:T(8,128)(2,1)} async-done(((bf16[96,768]{1,0:T(8,128)(2,1)}), bf16[768,768]{1,0:T(8,128)(2,1)}) %all-gather.23.cloned.1.call-update) | async-done | bytes 1179664 | tf_op jit(solution)/shard_map/all_gather | solution.py:29
  352.2 2.9 fusion.33
  355.2 0.3 all-gather.17.cloned.1.call-start
  355.5 2.0 fusion.4
  357.5 0.0 copy-done.18
  357.5 0.3 fusion.47
  357.8 0.0 copy-start.16
  357.9 2.0 fusion.6
  359.9 35.2 %all-gather.15.cloned.1.call-done = bf16[768,768]{1,0:T(8,128)(2,1)} async-done(((bf16[96,768]{1,0:T(8,128)(2,1)}), bf16[768,768]{1,0:T(8,128)(2,1)}) %all-gather.15.cloned.1.call-update) | async-done | bytes 1179664 | tf_op jit(solution)/shard_map/all_gather | solution.py:29
  395.1 2.5 fusion.31
  397.7 0.3 convolution_divide_fusion
  398.0 0.3 convolution_bitcast_fusion.1
  398.3 0.1 reshape.47
  398.4 12.5 %all_to_all.27 = f32[8,96,12]{1,2,0:T(8,128)S(1)} all-to-all(f32[8,96,12]{1,2,0:T(8,128)S(1)} %copy.23), channel_id=1, replica_groups=mesh['dp'=64,'mp'=8] {'mp'}, dimensions={0} | all-to-all | bytes 73728 | tf_op jit(solution)/shard_map/all_to_all | solution.py:43
  410.9 0.4 convolution_bitcast_fusion
  411.4 0.2 copy.25
  411.6 28.3 %all_to_all.28 = f32[64,12,96]{2,1,0:T(8,128)S(1)} all-to-all(f32[64,12,96]{2,1,0:T(8,128)S(1)} %reshape.48), channel_id=1, replica_groups=mesh['dp'=64,'mp'=8] {'dp'}, dimensions={0} | all-to-all | bytes 589824 | tf_op jit(solution)/shard_map/all_to_all | solution.py:43
  439.8 0.1 reduce_sum.57
  439.9 0.6 fusion.52
  440.6 17.9 %all_to_all.29 = bf16[64,12,96]{2,1,0:T(8,128)(2,1)S(1)} all-to-all(bf16[64,12,96]{2,1,0:T(8,128)(2,1)S(1)} %broadcast_in_dim.5), channel_id=1, replica_groups=mesh['dp'=64,'mp'=8] {'dp'}, dimensions={0} | all-to-all | bytes 294912 | tf_op jit(solution)/shard_map/all_to_all | solution.py:48
  458.5 0.1 reshape.49
  458.6 0.8 copy.26
  459.4 3.1 fusion.26
  462.5 18.4 %all-gather.17.cloned.1.call-done = bf16[768,768]{1,0:T(8,128)(2,1)} async-done(((bf16[96,768]{1,0:T(8,128)(2,1)}), bf16[768,768]{1,0:T(8,128)(2,1)}) %all-gather.17.cloned.1.call-update) | async-done | bytes 1179664 | tf_op jit(solution)/shard_map/all_gather | solution.py:29
  480.9 3.1 fusion.28
  (54 shorter events, 0.3 us)
Async XLA Ops:
  7.2 92.6 %all-gather.27.cloned.1.call-start = ((), (), s32[]{:S(2)}) async-start(), calls=%async_computation.13 | async-start | bytes 1597440 | tf_op jit(solution)/shard_map/all_gather | solution.py:59
  8.6 153.4 %all-gather.11.cloned.1.call-start = ((), (), s32[]{:S(2)}) async-start(), calls=%async_computation.5 | async-start | bytes 5308416 | tf_op jit(solution)/shard_map/all_gather | solution.py:60
  9.9 31.5 %copy-start.20 = (f32[12,96]{1,0:T(8,128)S(1)}, f32[12,96]{1,0:T(8,128)}, u32[]{:S(2)}) copy-start(f32[12,96]{1,0:T(8,128)} %param.10) | copy-start | bytes 13828
  41.4 29.1 %copy-start.17 = (f32[12,96]{1,0:T(8,128)}, f32[12,96]{1,0:T(8,128)S(1)}, u32[]{:S(2)}) copy-start(f32[12,96]{1,0:T(8,128)S(1)} %get-tuple-element.31) | copy-start | bytes 13828
  70.6 1.2 copy-start.1
  71.7 133.4 %all-gather.19.cloned.1.call-start = ((), (), s32[]{:S(2)}) async-start(), calls=%async_computation.9 | async-start | bytes 1327104 | tf_op jit(solution)/shard_map/all_gather | solution.py:61
  72.5 194.2 %all-gather.21.cloned.1.call-start = ((), (), s32[]{:S(2)}) async-start(), calls=%async_computation.10 | async-start | bytes 1327104 | tf_op jit(solution)/shard_map/all_gather | solution.py:29
  171.3 1.0 copy-start.14
  172.3 1.6 copy-start.3
  173.8 4.2 copy-start.10
  173.8 1.8 copy-start.15
  178.1 47.4 %copy-start.11 = (f32[96,768]{1,0:T(8,128)}, f32[96,768]{1,0:T(8,128)S(1)}, u32[]{:S(2)}) copy-start(f32[96,768]{1,0:T(8,128)S(1)} %fusion.20) | copy-start | bytes 884740
  205.1 21.1 %copy-start.12 = (f32[96,768]{1,0:T(8,128)S(1)}, f32[96,768]{1,0:T(8,128)}, u32[]{:S(2)}) copy-start(f32[96,768]{1,0:T(8,128)} %get-tuple-element.33) | copy-start | bytes 884740
  225.5 84.0 %all-gather.13.cloned.1.call-start = ((), (), s32[]{:S(2)}) async-start(), calls=%async_computation.6 | async-start | bytes 1327104 | tf_op jit(solution)/shard_map/all_gather | solution.py:29
  226.9 82.6 %copy-start.4 = (bf16[96,768]{1,0:T(8,128)(2,1)S(1)}, bf16[96,768]{1,0:T(8,128)(2,1)}, u32[]{:S(2)}) copy-start(bf16[96,768]{1,0:T(8,128)(2,1)} %multiply_convert_fusion.1) | copy-start | bytes 442372
  226.9 125.3 %all-gather.23.cloned.1.call-start = ((), (), s32[]{:S(2)}) async-start(), calls=%async_computation.11 | async-start | bytes 1327104 | tf_op jit(solution)/shard_map/all_gather | solution.py:29
  269.2 83.0 %copy-start.5 = (bf16[96,768]{1,0:T(8,128)(2,1)S(1)}, bf16[96,768]{1,0:T(8,128)(2,1)}, u32[]{:S(2)}) copy-start(bf16[96,768]{1,0:T(8,128)(2,1)} %multiply_convert_fusion) | copy-start | bytes 442372
  269.3 83.0 %copy-start.9 = (bf16[96,768]{1,0:T(8,128)(2,1)S(1)}, bf16[96,768]{1,0:T(8,128)(2,1)}, u32[]{:S(2)}) copy-start(bf16[96,768]{1,0:T(8,128)(2,1)} %convolution_convert_fusion.1) | copy-start | bytes 442372
  269.3 125.9 %all-gather.15.cloned.1.call-start = ((), (), s32[]{:S(2)}) async-start(), calls=%async_computation.7 | async-start | bytes 1327104 | tf_op jit(solution)/shard_map/all_gather | solution.py:29
  311.9 43.5 %copy-start.13 = (f32[768,12]{0,1:T(8,128)S(1)}, f32[768,12]{0,1:T(8,128)}, u32[]{:S(2)}) copy-start(f32[768,12]{0,1:T(8,128)} %param.12) | copy-start | bytes 110596
  312.0 147.4 %all-gather.25.cloned.1.call-start = ((), (), s32[]{:S(2)}) async-start(), calls=%async_computation.12 | async-start | bytes 1327104 | tf_op jit(solution)/shard_map/all_gather | solution.py:29
  355.2 2.4 copy-start.18
  355.2 125.8 %all-gather.17.cloned.1.call-start = ((), (), s32[]{:S(2)}) async-start(), calls=%async_computation.8 | async-start | bytes 1327104 | tf_op jit(solution)/shard_map/all_gather | solution.py:29
  355.4 2.4 copy-start
  357.8 39.9 %copy-start.16 = (f32[12,96]{1,0:T(8,128)}, f32[12,96]{1,0:T(8,128)S(1)}, u32[]{:S(2)}) copy-start(f32[12,96]{1,0:T(8,128)S(1)} %fusion.47) | copy-start | bytes 13828
  357.9 37.3 %copy-start.2 = (bf16[768,768]{1,0:T(8,128)(2,1)S(1)}, bf16[768,768]{1,0:T(8,128)(2,1)}, u32[]{:S(2)}) copy-start(bf16[768,768]{1,0:T(8,128)(2,1)} %all-gather.13.cloned.1.call-done) | copy-start | bytes 3538948
  357.9 37.2 %copy-start.8 = (bf16[96,768]{1,0:T(8,128)(2,1)S(1)}, bf16[96,768]{1,0:T(8,128)(2,1)}, u32[]{:S(2)}) copy-start(bf16[96,768]{1,0:T(8,128)(2,1)} %convolution_convert_fusion.3) | copy-start | bytes 442372
  411.5 28.4 %copy-start.19 = (f32[12,96]{1,0:T(8,128)S(1)}, f32[12,96]{1,0:T(8,128)}, u32[]{:S(2)}) copy-start(f32[12,96]{1,0:T(8,128)} %param.9) | copy-start | bytes 13828
  439.8 19.5 %copy-start.6 = (bf16[96,768]{1,0:T(8,128)(2,1)S(1)}, bf16[96,768]{1,0:T(8,128)(2,1)}, u32[]{:S(2)}) copy-start(bf16[96,768]{1,0:T(8,128)(2,1)} %fusion.33) | copy-start | bytes 442372
  459.4 21.5 %copy-start.7 = (bf16[96,768]{1,0:T(8,128)(2,1)S(1)}, bf16[96,768]{1,0:T(8,128)(2,1)}, u32[]{:S(2)}) copy-start(bf16[96,768]{1,0:T(8,128)(2,1)} %fusion.31) | copy-start | bytes 442372
Sparse Core Ops, SparseCore 0:
  11.9 87.7 all-gather.26
  101.8 60.1 all-gather.10
  164.7 40.3 all-gather.18
  225.6 41.0 all-gather.20
  269.2 40.2 all-gather.12
  312.0 40.2 all-gather.22
  354.9 40.2 all-gather.14
  397.8 40.2 all-gather.24
  440.7 40.1 all-gather.16
where the time goes:
time: 491 us
  waiting for transfers between devices  287 us (58%)
  blocking collectives  135 us (27%)
  matrix products  30.2 us (6%)
  local copies, waits for them, and re-layouts  16.3 us (3%)
  between operations  15.6 us (3%)
  other arithmetic  5.29 us (1%)
    all_gather x6, waiting for transfers between devices, all_rows(): lax.all_gather(for_sending(pair), 'mp', axis=0, tiled=True)  174 us
    all_to_all x3, blocking collectives, scatter_sum(): return jnp.sum(lax.all_to_all(chunks, axis, 0, 0, tiled=False), axis=0)  72.1 us
    all_gather x1, waiting for transfers between devices, per_device(): both_full = lax.all_gather(pieces, 'mp', axis=2, tiled=True)  59.1 us
    all_to_all x2, blocking collectives, gather_rows(): lax.all_to_all(jnp.broadcast_to(x[None], (count,) + x.shape), axis, 0, 0,...  46.8 us
    all_gather x1, waiting for transfers between devices, per_device(): right_full = lax.all_gather(right_basis, 'mp', axis=1, tiled=True)  27 us
    all_gather x1, waiting for transfers between devices, per_device(): left_full = lax.all_gather(left_basis, 'dp', axis=1, tiled=True)  27 us
    psum x1, blocking collectives, per_device(): lax.psum((jnp.sum(power_left * power_left), jnp.sum(power_right * power_r...  16.5 us
  transfers between devices with their start and end apart: 9, of which 8 were waited for; matrix products, arithmetic and copies ran while one was open for 9% of the time, Pallas kernels for 0%

commit v1 on v0

--- a/solution.py
+++ b/solution.py
@@ -13,6 +13,27 @@
 quint_b = -1.25
 quint_c = 0.375
 highest = lax.Precision.HIGHEST
+
+
+def collect(x, axis, dim):
+    count, index, rows = (lax.axis_size(axis), lax.axis_index(axis), x.shape[dim])
+    right = [(i, (i + 1) % count) for i in range(count)]
+    downward = [(i, (i - 1) % count) for i in range(count)]
+    out = jnp.zeros((*x.shape[:dim], count * rows, *x.shape[dim + 1 :]), x.dtype)
+    out = lax.dynamic_update_slice_in_dim(out, x, index * rows, axis=dim)
+    from_left = from_right = x
+    middle = count // 2
+    for hop in range(1, middle + 1):
+        from_left = lax.ppermute(from_left, axis, right)
+        out = lax.dynamic_update_slice_in_dim(
+            out, from_left, (index - hop) % count * rows, axis=dim
+        )
+        if hop < count - middle:
+            from_right = lax.ppermute(from_right, axis, downward)
+            out = lax.dynamic_update_slice_in_dim(
+                out, from_right, (index + hop) % count * rows, axis=dim
+            )
+    return out
 
 
 def for_sending(x):
@@ -58,7 +79,7 @@
     pieces = jnp.swapaxes(pieces, 0, 1).reshape(2, -1, pieces.shape[-1])
     left_full = lax.all_gather(left_basis, "dp", axis=1, tiled=True)
     both_full = lax.all_gather(pieces, "mp", axis=2, tiled=True)
-    right_full = lax.all_gather(right_basis, "mp", axis=1, tiled=True)
+    right_full = collect(right_basis, "mp", 1)
     grad_full = both_full[0]
     moment_full = both_full[1]
 

time: 491 us -> 464 us (0.945)
  waiting for transfers between devices: 287 us -> 234 us
  starting transfers between devices: 0.77 us -> 24 us
    all_gather x1 -> x0, waiting for transfers between devices: 27 us -> none  [per_device(): right_full = lax.all_gather(right_basis, 'mp', axis=1, tiled=True)]
    all_gather x1, waiting for transfers between devices: 27 us -> 0.02 us  [per_device(): left_full = lax.all_gather(left_basis, 'dp', axis=1, tiled=True)]
    ppermute x0 -> x7, starting transfers between devices: none -> 23.4 us  [the longest x3 14.1 us: collect(): from_right = lax.ppermute(from_right, axis, downward)]
    ppermute x0 -> x7, waiting for transfers between devices: none -> 9.66 us  [the longest x4 9.66 us: collect(): from_left = lax.ppermute(from_left, axis, right)]
    all_gather x1, waiting for transfers between devices: 59.1 us -> 52.7 us  [per_device(): both_full = lax.all_gather(pieces, 'mp', axis=2, tiled=True)]
  transfers between devices with their start and end apart: 9 -> 15, of which waited for: 8 -> 10; matrix products, arithmetic and copies ran while one was open for 9% -> 6% of each run, Pallas kernels for 0% -> 0%
where the time goes in v1:
time: 464 us; the launch traced here: 463 us
  waiting for transfers between devices  234 us (50%)
  blocking collectives  135 us (29%)
  matrix products  30.4 us (7%)
  starting transfers between devices  24 us (5%)
  local copies, waits for them, and re-layouts  17.3 us (4%)
  between operations  16.1 us (3%)
  other arithmetic  6.54 us (1%)
    all_gather x6, waiting for transfers between devices, all_rows(): lax.all_gather(for_sending(pair), 'mp', axis=0, tiled=True)  171 us
    all_to_all x3, blocking collectives, scatter_sum(): return jnp.sum(lax.all_to_all(chunks, axis, 0, 0, tiled=False), axis=0)  72.1 us
    all_gather x1, waiting for transfers between devices, per_device(): both_full = lax.all_gather(pieces, 'mp', axis=2, tiled=True)  52.7 us
    all_to_all x2, blocking collectives, gather_rows(): lax.all_to_all(jnp.broadcast_to(x[None], (count,) + x.shape), axis, 0, 0,...  46.8 us
    psum x1, blocking collectives, per_device(): lax.psum((jnp.sum(power_left * power_left), jnp.sum(power_right * power_r...  16.2 us
    ppermute x3, starting transfers between devices, collect(): from_right = lax.ppermute(from_right, axis, downward)  14.1 us
    ppermute x4, waiting for transfers between devices, collect(): from_left = lax.ppermute(from_left, axis, right)  9.66 us
    ppermute x4, starting transfers between devices, collect(): from_left = lax.ppermute(from_left, axis, right)  9.38 us
  transfers between devices with their start and end apart: 15, of which 10 were waited for; matrix products, arithmetic and copies ran while one was open for 6% of the time, Pallas kernels for 0%

profile of v1, /device:TPU:2, one launch (start us, length us, event | category | flops | bytes accessed | tf_op | source)
XLA Modules:
  0.0 463.1 jit_solution(7791195882344587852)
XLA Ops:
  7.2 1.4 bitcast_convert_fusion
  8.7 1.0 convert_reduce_fusion
  9.7 0.2 copy.20
  10.0 31.4 %all_to_all.25 = f32[64,12,96]{2,1,0:T(8,128)S(1)} all-to-all(f32[64,12,96]{2,1,0:T(8,128)S(1)} %reshape.45), channel_id=1, replica_groups=mesh['dp'=64,'mp'=8] {'dp'}, dimensions={0} | all-to-all | bytes 589824 | tf_op jit(solution)/shard_map/all_to_all | solution.py:64
  41.3 0.1 reduce_sum.55
  41.5 0.2 broadcast_in_dim.6
  41.7 28.9 %all_to_all.26 = f32[64,2,12,96]{3,1,2,0:T(2,128)S(1)} all-to-all(f32[64,2,12,96]{3,1,2,0:T(2,128)S(1)} %broadcast_in_dim.6), channel_id=1, replica_groups=mesh['dp'=64,'mp'=8] {'dp'}, dimensions={0} | all-to-all | bytes 1179648 | tf_op jit(solution)/shard_map/all_to_all | solution.py:69
  70.6 1.1 copy.22
  71.8 0.1 broadcast_in_dim.8
  71.8 0.8 copy-done.1
  72.7 3.5 collective-permute-start
  76.1 3.8 collective-permute-start.1
  80.1 1.3 collective-permute-done
  81.4 1.9 collective-permute-start.2
  83.3 5.1 %collective-permute-start.3 = (bf16[768,96]{0,1:T(8,128)(2,1)S(1)}, bf16[768,96]{0,1:T(8,128)(2,1)S(1)}, u32[]{:S(2)}, u32[]{:S(2)}) collective-permute-start(bf16[768,96]{0,1:T(8,128)(2,1)S(1)} %collective-permute-done.1), channel_id=1, source_target_pairs={{0,7},{1,0},{2,1},{3,2},{4,3},{5,4},{6,5},{7,6},{8,15},{9,8},{10,9... | collective-permute-start | bytes 442376 | tf_op jit(solution)/shard_map/ppermute | solution.py:32
  88.5 1.1 collective-permute-done.2
  89.7 1.9 collective-permute-start.4
  91.6 5.1 %collective-permute-start.5 = (bf16[768,96]{0,1:T(8,128)(2,1)S(1)}, bf16[768,96]{0,1:T(8,128)(2,1)S(1)}, u32[]{:S(2)}, u32[]{:S(2)}) collective-permute-start(bf16[768,96]{0,1:T(8,128)(2,1)S(1)} %collective-permute-done.3), channel_id=1, source_target_pairs={{0,7},{1,0},{2,1},{3,2},{4,3},{5,4},{6,5},{7,6},{8,15},{9,8},{10,9... | collective-permute-start | bytes 442376 | tf_op jit(solution)/shard_map/ppermute | solution.py:32
  96.8 1.1 collective-permute-done.4
  97.9 2.1 collective-permute-start.6
  100.0 6.1 %collective-permute-done.6 = bf16[768,96]{0,1:T(8,128)(2,1)S(1)} collective-permute-done((bf16[768,96]{0,1:T(8,128)(2,1)S(1)}, bf16[768,96]{0,1:T(8,128)(2,1)S(1)}, u32[]{:S(2)}, u32[]{:S(2)}) %collective-permute-start.6) | collective-permute-done | bytes 147488 | tf_op jit(solution)/shard_map/ppermute | solution.py:27
  106.2 3.1 reshape.52
  109.3 52.7 %all-gather.10.cloned.1.call-done = f32[2,768,768]{1,0,2:T(2,128)} async-done(((f32[2,768,96]{1,0,2:T(2,128)}), f32[2,768,768]{1,0,2:T(2,128)}) %all-gather.10.cloned.1.call-update) | async-done | bytes 4718608 | tf_op jit(solution)/shard_map/all_gather | solution.py:81
  162.0 9.3 %fusion.53 = (f32[1,768,768]{1,0,2:T(1,128)S(1)}, f32[1,768,768]{1,0,2:T(1,128)}) fusion(f32[2,768,768]{1,0,2:T(2,128)} %all-gather.10.cloned.1.call-done), kind=kLoop, calls=%fused_computation.78 | loop fusion | bytes 9437184 | tf_op jit(solution)/shard_map/slice | solution.py:83
  171.3 0.9 constant_dynamic-slice_fusion.1
  172.2 0.1 constant_dynamic-slice_fusion
  172.3 1.5 fusion.23
  173.8 2.4 fusion.20
  176.3 1.8 multiply_reduce_fusion.1
  178.1 1.8 multiply_reduce_fusion
  179.9 16.2 %all-reduce = (f32[]{:T(128)}, f32[]{:T(128)}) all-reduce(f32[]{:T(128)} %get-tuple-element.35, f32[]{:T(128)} %get-tuple-element.37), channel_id=1, replica_groups=mesh['dp'=64,'mp'=8] {'mp'}, use_global_device_ids=true, to_apply=%region_5.6 | all-reduce | flops 2 | bytes 16 | tf_op jit(solution)/shard_map/psum | solution.py:125
  196.8 1.6 multiply_convert_fusion.1
  199.2 1.6 multiply_convert_fusion
  200.9 0.0 all-gather.14.cloned.1.call-start
  200.9 39.3 %all-gather.12.cloned.1.call-done = bf16[768,768]{1,0:T(8,128)(2,1)} async-done(((bf16[96,768]{1,0:T(8,128)(2,1)}), bf16[768,768]{1,0:T(8,128)(2,1)}) %all-gather.12.cloned.1.call-update) | async-done | bytes 1179664 | tf_op jit(solution)/shard_map/all_gather | solution.py:50
  240.2 2.5 convolution_convert_fusion.3
  242.8 0.0 all-gather.20.cloned.1.call-start
  242.8 39.6 %all-gather.18.cloned.1.call-done = bf16[768,768]{1,0:T(8,128)(2,1)} async-done(((bf16[96,768]{1,0:T(8,128)(2,1)}), bf16[768,768]{1,0:T(8,128)(2,1)}) %all-gather.18.cloned.1.call-update) | async-done | bytes 1179664 | tf_op jit(solution)/shard_map/all_gather | solution.py:50
  282.4 2.5 convolution_convert_fusion.1
  284.9 0.0 all-gather.16.cloned.1.call-start
  285.0 40.2 %all-gather.14.cloned.1.call-done = bf16[768,768]{1,0:T(8,128)(2,1)} async-done(((bf16[96,768]{1,0:T(8,128)(2,1)}), bf16[768,768]{1,0:T(8,128)(2,1)}) %all-gather.14.cloned.1.call-update) | async-done | bytes 1179664 | tf_op jit(solution)/shard_map/all_gather | solution.py:50
  325.2 2.6 fusion.31
  327.8 0.3 all-gather.22.cloned.1.call-start
  328.1 3.0 fusion.4
  331.1 0.3 fusion.47
  331.4 0.0 copy-start.16
  331.5 2.0 fusion.6
  333.6 33.8 %all-gather.20.cloned.1.call-done = bf16[768,768]{1,0:T(8,128)(2,1)} async-done(((bf16[96,768]{1,0:T(8,128)(2,1)}), bf16[768,768]{1,0:T(8,128)(2,1)}) %all-gather.20.cloned.1.call-update) | async-done | bytes 1179664 | tf_op jit(solution)/shard_map/all_gather | solution.py:50
  367.3 2.5 fusion.33
  369.9 0.3 convolution_divide_fusion
  370.2 0.3 convolution_bitcast_fusion.1
  370.5 0.1 reshape.47
  370.6 12.5 %all_to_all.27 = f32[8,96,12]{1,2,0:T(8,128)S(1)} all-to-all(f32[8,96,12]{1,2,0:T(8,128)S(1)} %copy.23), channel_id=1, replica_groups=mesh['dp'=64,'mp'=8] {'mp'}, dimensions={0} | all-to-all | bytes 73728 | tf_op jit(solution)/shard_map/all_to_all | solution.py:64
  383.1 0.4 convolution_bitcast_fusion
  383.6 0.2 copy.25
  383.8 28.3 %all_to_all.28 = f32[64,12,96]{2,1,0:T(8,128)S(1)} all-to-all(f32[64,12,96]{2,1,0:T(8,128)S(1)} %reshape.48), channel_id=1, replica_groups=mesh['dp'=64,'mp'=8] {'dp'}, dimensions={0} | all-to-all | bytes 589824 | tf_op jit(solution)/shard_map/all_to_all | solution.py:64
  412.1 0.1 reduce_sum.57
  412.2 0.6 fusion.52
  412.8 17.9 %all_to_all.29 = bf16[64,12,96]{2,1,0:T(8,128)(2,1)S(1)} all-to-all(bf16[64,12,96]{2,1,0:T(8,128)(2,1)S(1)} %broadcast_in_dim.7), channel_id=1, replica_groups=mesh['dp'=64,'mp'=8] {'dp'}, dimensions={0} | all-to-all | bytes 294912 | tf_op jit(solution)/shard_map/all_to_all | solution.py:69
  430.7 0.1 reshape.49
  430.8 0.8 copy.26
  431.6 3.1 fusion.28
  434.7 18.4 %all-gather.22.cloned.1.call-done = bf16[768,768]{1,0:T(8,128)(2,1)} async-done(((bf16[96,768]{1,0:T(8,128)(2,1)}), bf16[768,768]{1,0:T(8,128)(2,1)}) %all-gather.22.cloned.1.call-update) | async-done | bytes 1179664 | tf_op jit(solution)/shard_map/all_gather | solution.py:50
  453.1 3.1 fusion.26
  (73 shorter events, 0.7 us)
Async XLA Ops:
  7.2 99.0 %all-gather.24.cloned.1.call-start = ((), (), s32[]{:S(2)}) async-start(), calls=%async_computation.12 | async-start | bytes 1597440 | tf_op jit(solution)/shard_map/all_gather | solution.py:80
  8.6 153.4 %all-gather.10.cloned.1.call-start = ((), (), s32[]{:S(2)}) async-start(), calls=%async_computation.5 | async-start | bytes 5308416 | tf_op jit(solution)/shard_map/all_gather | solution.py:81
  9.9 31.5 %copy-start.20 = (f32[12,96]{1,0:T(8,128)S(1)}, f32[12,96]{1,0:T(8,128)}, u32[]{:S(2)}) copy-start(f32[12,96]{1,0:T(8,128)} %param.10) | copy-start | bytes 13828
  41.4 29.1 %copy-start.17 = (f32[12,96]{1,0:T(8,128)}, f32[12,96]{1,0:T(8,128)S(1)}, u32[]{:S(2)}) copy-start(f32[12,96]{1,0:T(8,128)S(1)} %get-tuple-element.34) | copy-start | bytes 13828
  71.7 1.0 copy-start.1
  71.7 168.5 %all-gather.12.cloned.1.call-start = ((), (), s32[]{:S(2)}) async-start(), calls=%async_computation.6 | async-start | bytes 1327104 | tf_op jit(solution)/shard_map/all_gather | solution.py:50
  72.7 8.8 %collective-permute-start = (bf16[768,96]{0,1:T(8,128)(2,1)S(1)}, bf16[768,96]{0,1:T(8,128)(2,1)S(1)}, u32[]{:S(2)}, u32[]{:S(2)}) collective-permute-start(bf16[768,96]{0,1:T(8,128)(2,1)S(1)} %get-tuple-element.30), channel_id=1, source_target_pairs={{0,1},{1,2},{2,3},{3,4},{4,5},{5,6},{6,7},{7,0},{8,9},{9,10},{10,1... | collective-permute-start | bytes 442376 | tf_op jit(solution)/shard_map/ppermute | solution.py:27
  76.1 7.2 %collective-permute-start.1 = (bf16[768,96]{0,1:T(8,128)(2,1)S(1)}, bf16[768,96]{0,1:T(8,128)(2,1)S(1)}, u32[]{:S(2)}, u32[]{:S(2)}) collective-permute-start(bf16[768,96]{0,1:T(8,128)(2,1)S(1)} %get-tuple-element.30), channel_id=1, source_target_pairs={{0,7},{1,0},{2,1},{3,2},{4,3},{5,4},{6,5},{7,6},{8,15},{9,8},{10,9... | collective-permute-start | bytes 442376 | tf_op jit(solution)/shard_map/ppermute | solution.py:32
  81.4 8.2 %collective-permute-start.2 = (bf16[768,96]{0,1:T(8,128)(2,1)S(1)}, bf16[768,96]{0,1:T(8,128)(2,1)S(1)}, u32[]{:S(2)}, u32[]{:S(2)}) collective-permute-start(bf16[768,96]{0,1:T(8,128)(2,1)S(1)} %collective-permute-done), channel_id=1, source_target_pairs={{0,1},{1,2},{2,3},{3,4},{4,5},{5,6},{6,7},{7,0},{8,9},{9,10},{10,1... | collective-permute-start | bytes 442376 | tf_op jit(solution)/shard_map/ppermute | solution.py:27
  83.3 8.2 %collective-permute-start.3 = (bf16[768,96]{0,1:T(8,128)(2,1)S(1)}, bf16[768,96]{0,1:T(8,128)(2,1)S(1)}, u32[]{:S(2)}, u32[]{:S(2)}) collective-permute-start(bf16[768,96]{0,1:T(8,128)(2,1)S(1)} %collective-permute-done.1), channel_id=1, source_target_pairs={{0,7},{1,0},{2,1},{3,2},{4,3},{5,4},{6,5},{7,6},{8,15},{9,8},{10,9... | collective-permute-start | bytes 442376 | tf_op jit(solution)/shard_map/ppermute | solution.py:32
  89.7 8.2 %collective-permute-start.4 = (bf16[768,96]{0,1:T(8,128)(2,1)S(1)}, bf16[768,96]{0,1:T(8,128)(2,1)S(1)}, u32[]{:S(2)}, u32[]{:S(2)}) collective-permute-start(bf16[768,96]{0,1:T(8,128)(2,1)S(1)} %collective-permute-done.2), channel_id=1, source_target_pairs={{0,1},{1,2},{2,3},{3,4},{4,5},{5,6},{6,7},{7,0},{8,9},{9,10},{10,1... | collective-permute-start | bytes 442376 | tf_op jit(solution)/shard_map/ppermute | solution.py:27
  91.6 8.4 %collective-permute-start.5 = (bf16[768,96]{0,1:T(8,128)(2,1)S(1)}, bf16[768,96]{0,1:T(8,128)(2,1)S(1)}, u32[]{:S(2)}, u32[]{:S(2)}) collective-permute-start(bf16[768,96]{0,1:T(8,128)(2,1)S(1)} %collective-permute-done.3), channel_id=1, source_target_pairs={{0,7},{1,0},{2,1},{3,2},{4,3},{5,4},{6,5},{7,6},{8,15},{9,8},{10,9... | collective-permute-start | bytes 442376 | tf_op jit(solution)/shard_map/ppermute | solution.py:32
  97.9 8.2 %collective-permute-start.6 = (bf16[768,96]{0,1:T(8,128)(2,1)S(1)}, bf16[768,96]{0,1:T(8,128)(2,1)S(1)}, u32[]{:S(2)}, u32[]{:S(2)}) collective-permute-start(bf16[768,96]{0,1:T(8,128)(2,1)S(1)} %collective-permute-done.4), channel_id=1, source_target_pairs={{0,1},{1,2},{2,3},{3,4},{4,5},{5,6},{6,7},{7,0},{8,9},{9,10},{10,1... | collective-permute-start | bytes 442376 | tf_op jit(solution)/shard_map/ppermute | solution.py:27
  171.3 1.0 copy-start.14
  172.3 1.6 copy-start.15
  173.8 2.4 copy-start.10
  173.8 2.4 copy-start.5
  176.3 3.6 copy-start.11
  198.5 83.9 %all-gather.18.cloned.1.call-start = ((), (), s32[]{:S(2)}) async-start(), calls=%async_computation.9 | async-start | bytes 1327104 | tf_op jit(solution)/shard_map/all_gather | solution.py:50
  200.9 124.3 %all-gather.14.cloned.1.call-start = ((), (), s32[]{:S(2)}) async-start(), calls=%async_computation.7 | async-start | bytes 1327104 | tf_op jit(solution)/shard_map/all_gather | solution.py:50
  242.7 82.4 %copy-start.4 = (bf16[768,768]{1,0:T(8,128)(2,1)S(1)}, bf16[768,768]{1,0:T(8,128)(2,1)}, u32[]{:S(2)}) copy-start(bf16[768,768]{1,0:T(8,128)(2,1)} %all-gather.12.cloned.1.call-done) | copy-start | bytes 3538948
  242.8 124.6 %all-gather.20.cloned.1.call-start = ((), (), s32[]{:S(2)}) async-start(), calls=%async_computation.10 | async-start | bytes 1327104 | tf_op jit(solution)/shard_map/all_gather | solution.py:50
  284.9 146.7 %all-gather.16.cloned.1.call-start = ((), (), s32[]{:S(2)}) async-start(), calls=%async_computation.8 | async-start | bytes 1327104 | tf_op jit(solution)/shard_map/all_gather | solution.py:50
  327.8 3.3 copy-start.2
  327.8 3.3 copy-start.18
  327.8 125.3 %all-gather.22.cloned.1.call-start = ((), (), s32[]{:S(2)}) async-start(), calls=%async_computation.11 | async-start | bytes 1327104 | tf_op jit(solution)/shard_map/all_gather | solution.py:50
  328.1 3.4 copy-start
  328.1 3.4 copy-start.12
  331.4 38.5 %copy-start.16 = (f32[12,96]{1,0:T(8,128)}, f32[12,96]{1,0:T(8,128)S(1)}, u32[]{:S(2)}) copy-start(f32[12,96]{1,0:T(8,128)S(1)} %fusion.47) | copy-start | bytes 13828
  331.5 35.8 %copy-start.3 = (bf16[768,768]{1,0:T(8,128)(2,1)S(1)}, bf16[768,768]{1,0:T(8,128)(2,1)}, u32[]{:S(2)}) copy-start(bf16[768,768]{1,0:T(8,128)(2,1)} %all-gather.18.cloned.1.call-done) | copy-start | bytes 3538948
  331.5 35.8 %copy-start.6 = (bf16[96,768]{1,0:T(8,128)(2,1)S(1)}, bf16[96,768]{1,0:T(8,128)(2,1)}, u32[]{:S(2)}) copy-start(bf16[96,768]{1,0:T(8,128)(2,1)} %multiply_convert_fusion) | copy-start | bytes 442372
  331.5 35.8 %copy-start.9 = (bf16[96,768]{1,0:T(8,128)(2,1)S(1)}, bf16[96,768]{1,0:T(8,128)(2,1)}, u32[]{:S(2)}) copy-start(bf16[96,768]{1,0:T(8,128)(2,1)} %convolution_convert_fusion.1) | copy-start | bytes 442372
  369.9 13.2 %copy-start.13 = (f32[768,12]{0,1:T(8,128)S(1)}, f32[768,12]{0,1:T(8,128)}, u32[]{:S(2)}) copy-start(f32[768,12]{0,1:T(8,128)} %param.12) | copy-start | bytes 110596
  383.7 28.4 %copy-start.19 = (f32[12,96]{1,0:T(8,128)S(1)}, f32[12,96]{1,0:T(8,128)}, u32[]{:S(2)}) copy-start(f32[12,96]{1,0:T(8,128)} %param.9) | copy-start | bytes 13828
  412.1 19.5 %copy-start.7 = (bf16[96,768]{1,0:T(8,128)(2,1)S(1)}, bf16[96,768]{1,0:T(8,128)(2,1)}, u32[]{:S(2)}) copy-start(bf16[96,768]{1,0:T(8,128)(2,1)} %fusion.31) | copy-start | bytes 442372
  431.6 21.5 %copy-start.8 = (bf16[96,768]{1,0:T(8,128)(2,1)S(1)}, bf16[96,768]{1,0:T(8,128)(2,1)}, u32[]{:S(2)}) copy-start(bf16[96,768]{1,0:T(8,128)(2,1)} %fusion.33) | copy-start | bytes 442372
Sparse Core Ops, SparseCore 0:
  11.9 87.7 all-gather.23
  101.8 60.2 all-gather.9
  198.6 41.5 all-gather.11
  242.2 40.2 all-gather.17
  284.9 40.2 all-gather.13
  327.1 40.2 all-gather.19
  370.0 40.2 all-gather.15
  412.9 40.1 all-gather.21
